TPU v7x, 512 devices: a whole 4x8x8 slice. The times are simulated.
512 devices in a mesh: dp: 4 (over x), seq: 16 (over z, core), head: 8 (over y).
Axes of the slice: x: 4, y: 8, z: 8, core: 2. Of those that a mesh axis runs over, the one named last changes fastest.
Arguments:
- doc_ids: int32 [16384], P(('dp', 'seq')), parts along dimension 0, may hold values from 0 to 7, never falling along the last dimension, each value on 1 to 2048 neighbouring positions
- light_q: bfloat16 [16384, 4096], P(('dp', 'seq'), 'head'), parts along dimension 0, may hold values from -0.59765625 to 0.59765625
- light_k: bfloat16 [16384, 4096], P(('dp', 'seq'), 'head'), parts along dimension 0, may hold values from -0.59765625 to 0.59765625
- light_v: bfloat16 [16384, 4096], P(('dp', 'seq'), 'head'), parts along dimension 0, may hold values from -6 to 6
- light_decay: float32 [32], P('head'), may hold values from 0 to 1
- light_grad_out: bfloat16 [16384, 4096], P(('dp', 'seq'), 'head'), parts along dimension 0, may hold values from -6 to 6
- soft_q: bfloat16 [16384, 4096], P(('dp', 'seq'), 'head'), parts along dimension 0, may hold values from -40 to 40
- soft_k: bfloat16 [16384, 4096], P(('dp', 'seq'), 'head'), parts along dimension 0, may hold values from -40 to 40
- soft_v: bfloat16 [16384, 4096], P(('dp', 'seq'), 'head'), parts along dimension 0, may hold values from -6 to 6
- soft_grad_out: bfloat16 [16384, 4096], P(('dp', 'seq'), 'head'), parts along dimension 0, may hold values from -6 to 6
Outputs:
- lightning_output: bfloat16 [16384, 4096], P(('dp', 'seq'), 'head'), parts along dimension 0
- lightning_query_gradient: bfloat16 [16384, 4096], P(('dp', 'seq'), 'head'), parts along dimension 0
- lightning_key_gradient: bfloat16 [16384, 4096], P(('dp', 'seq'), 'head'), parts along dimension 0
- lightning_value_gradient: bfloat16 [16384, 4096], P(('dp', 'seq'), 'head'), parts along dimension 0
- soft_out: bfloat16 [16384, 4096], P(('dp', 'seq'), 'head'), parts along dimension 0
- soft_dq: bfloat16 [16384, 4096], P(('dp', 'seq'), 'head'), parts along dimension 0
- soft_dk: bfloat16 [16384, 4096], P(('dp', 'seq'), 'head'), parts along dimension 0
- soft_dv: bfloat16 [16384, 4096], P(('dp', 'seq'), 'head'), parts along dimension 0
There are 4 independent parts, one for each index of `dp`. A program takes and returns all parts, laid end to end along the dimension named above; an argument that names none is the same for every part. Nothing has to cross between parts.
Inputs may be any that keep to these rules, and one draw needn't show every extreme that they name: `doc_ids`: document ids never fall along the sequence; each document holds at most 2048 tokens, and one holds exactly that many.
All inputs are finite; a program needn't handle non-finite values.
Results may differ from a plain program's by a relative error of at most 0.02.
Values may be sent and summed in bfloat16 or wider, within the bound.
No kernel may reach another device: no remote copies, remote signals or barrier semaphores. Data moves between devices by JAX's collectives and lax.ppermute only.
A program may use at most 128 MiB of HBM per device.

v0:
```python
import jax
import jax.numpy as jnp
from jax import lax
from jax.sharding import PartitionSpec as P

PRECISE = lax.Precision.HIGH


def entering(part, axis, combine, identity, reverse):
    count = lax.axis_size(axis)
    place = lax.axis_index(axis)
    ahead = count - 1 - place if reverse else place
    gathered = jax.tree.map(lambda a: lax.all_gather(a, axis), part)
    state = jax.tree.map(lambda a, e: jnp.zeros_like(a) + jnp.asarray(e, a.dtype), part, identity)

    def one(lap, state):
        source = count - 1 - lap if reverse else lap
        return combine(
            state, jax.tree.map(lambda a: lax.dynamic_index_in_dim(a, source, 0, False), gathered)
        )

    return lax.fori_loop(0, ahead, one, state)


def from_behind(value, axis, steps):
    count = lax.axis_size(axis)
    first, last = (max(0, -steps), min(count, count - steps))
    return lax.ppermute(value, axis, [(source, source + steps) for source in range(first, last)])


def join_forward(earlier, later):
    state_a, keep_a, head_a, tail_a = earlier
    state_b, keep_b, head_b, tail_b = later
    empty_a = tail_a < 0
    empty_b = tail_b < 0
    joined = (head_b == tail_b) & (head_b == tail_a)
    running_state = jnp.where(
        empty_b, state_a, jnp.where(joined, keep_b[:, None, None] * state_a + state_b, state_b)
    )
    return (
        running_state,
        keep_a * keep_b,
        jnp.where(empty_a, head_b, head_a),
        jnp.where(empty_b, tail_a, tail_b),
    )


def join_backward(earlier, later):
    state_h, keep_h, head_h, tail_h = earlier
    state_l, keep_l, head_l, tail_l = later
    empty_h = tail_h < 0
    empty_l = tail_l < 0
    joined = (head_l == tail_l) & (tail_l == head_h)
    running_state = jnp.where(
        empty_l, state_h, jnp.where(joined, keep_l[:, None, None] * state_h + state_l, state_l)
    )
    return (
        running_state,
        keep_h * keep_l,
        jnp.where(empty_l, head_h, head_l),
        jnp.where(empty_h, tail_l, tail_h),
    )


def mixed_result(form, left, right):
    return jnp.einsum(form, left, right, precision=PRECISE, preferred_element_type=jnp.float32)


def per_device(
    doc_ids,
    light_q,
    light_k,
    light_v,
    light_decay,
    light_grad_out,
    soft_q,
    soft_k,
    soft_v,
    soft_grad_out,
):
    tok_rows = light_q.shape[0]
    heads = light_decay.shape[0]
    width = light_q.shape[1] // heads
    shards = lax.axis_size("seq")
    total_rows = tok_rows * shards
    offset = lax.axis_index("seq") * tok_rows
    last_pos = offset + tok_rows - 1
    all_ids = lax.all_gather(doc_ids, "seq", axis=0, tiled=True)
    positions = offset + jnp.arange(tok_rows, dtype=jnp.int32)
    own_ids = doc_ids.astype(jnp.float32)
    within_segment_position = jnp.arange(tok_rows, dtype=jnp.int32)
    reach = min(shards - 1, (tok_rows + total_rows // 2 - 2) // tok_rows)
    query_half_rows = light_q.reshape(tok_rows, heads, width)
    key_half_rows = light_k.reshape(tok_rows, heads, width)
    value_half_rows = light_v.reshape(tok_rows, heads, width)
    backward_sequence_share = light_grad_out.reshape(tok_rows, heads, width)
    inside = (doc_ids[:, None] == doc_ids[None, :]) & (
        within_segment_position[None, :] <= within_segment_position[:, None]
    )
    distance = jnp.maximum(
        within_segment_position[:, None] - within_segment_position[None, :], 0
    ).astype(jnp.float32)
    weight = jnp.where(inside[None], jnp.exp(-light_decay[:, None, None] * distance[None]), 0.0)
    scores = (
        jnp.einsum(
            "thd,shd->hts", query_half_rows, key_half_rows, preferred_element_type=jnp.float32
        )
        * weight
    )
    lightning_output = mixed_result("hts,shd->thd", scores, value_half_rows)
    head_id = own_ids[0]
    tail_id = own_ids[-1]
    since_start = (within_segment_position + 1).astype(jnp.float32)
    until_end = (tok_rows - 1 - within_segment_position).astype(jnp.float32)
    start_decay = jnp.exp(-since_start[:, None] * light_decay[None, :])
    end_decay = jnp.exp(-until_end[:, None] * light_decay[None, :])
    offset_to_end = end_decay * (own_ids == tail_id)[:, None]
    running_state = mixed_result(
        "bto,btq->toq", key_half_rows * offset_to_end[:, :, None], value_half_rows
    )
    keep = jnp.exp(-light_decay * tok_rows)
    identity = (
        jnp.zeros_like(running_state),
        jnp.ones_like(keep),
        jnp.float32(-1.0),
        jnp.float32(-1.0),
    )
    inherited_memory_matrix, _, _, carried_id = entering(
        (running_state, keep, head_id, tail_id), "seq", join_forward, identity, False
    )
    distance_since_beginning = start_decay * (own_ids == carried_id)[:, None]
    lightning_output = lightning_output + mixed_result(
        "peb,ebi->pei",
        query_half_rows * distance_since_beginning[:, :, None],
        inherited_memory_matrix,
    )
    grad_scores = (
        jnp.einsum(
            "thv,shv->hts",
            backward_sequence_share,
            value_half_rows,
            preferred_element_type=jnp.float32,
        )
        * weight
    )
    lightning_query_gradient = mixed_result("hts,shk->thk", grad_scores, key_half_rows)
    lightning_query_gradient = lightning_query_gradient + mixed_result(
        "mcq,cxq->mcx",
        backward_sequence_share * distance_since_beginning[:, :, None],
        inherited_memory_matrix,
    )
    lightning_key_gradient = mixed_result("hts,thk->shk", grad_scores, query_half_rows)
    lightning_value_gradient = mixed_result("hts,thv->shv", scores, backward_sequence_share)
    opening_part = start_decay * (own_ids == head_id)[:, None]
    pending_state = mixed_result(
        "ejn,ejf->jnf", query_half_rows * opening_part[:, :, None], backward_sequence_share
    )
    returned_value, _, yielded_document_number, _ = entering(
        (pending_state, keep, head_id, tail_id), "seq", join_backward, identity, True
    )
    closing_part = (end_decay * (own_ids == yielded_document_number)[:, None])[:, :, None]
    lightning_key_gradient = (
        lightning_key_gradient
        + mixed_result("qpb,aqb->aqp", returned_value, value_half_rows) * closing_part
    )
    lightning_value_gradient = (
        lightning_value_gradient
        + mixed_result("dgp,zdg->zdp", returned_value, key_half_rows) * closing_part
    )
    scale = width ** (-0.5)
    soft_query = soft_q.reshape(tok_rows, heads, width)
    soft_grads = soft_grad_out.reshape(tok_rows, heads, width)
    soft_keys = soft_k.reshape(tok_rows, heads, width)
    soft_values = soft_v.reshape(tok_rows, heads, width)
    all_keys, all_values = (
        lax.all_gather(soft_k, "seq", axis=0, tiled=True),
        lax.all_gather(soft_v, "seq", axis=0, tiled=True),
    )
    first_pos = jnp.sum(all_ids < doc_ids[0])
    doc_end = jnp.sum(all_ids <= doc_ids[-1]) - 1
    key_block = min(512, total_rows)
    key_count = total_rows // key_block
    block_order = jnp.arange(key_count, dtype=jnp.int32)

    def key_mask(start, count):
        key_pos = start + jnp.arange(count, dtype=jnp.int32)
        key_ids = lax.dynamic_slice_in_dim(all_ids, start, count)
        return (key_pos[None, :] <= positions[:, None]) & (key_ids[None, :] == doc_ids[:, None])

    def held_block(start):
        segment_attention_inputs = lax.dynamic_slice_in_dim(all_keys, start, key_block).reshape(
            key_block, heads, width
        )
        block_values = lax.dynamic_slice_in_dim(all_values, start, key_block).reshape(
            key_block, heads, width
        )
        return (segment_attention_inputs, block_values)

    def unused(start):
        return (start > last_pos) | (start + key_block - 1 < first_pos)

    def forward_block(carry, index):
        start = index * key_block

        def forward_update(inner):
            top, total, accum = inner
            segment_attention_inputs, block_values = held_block(start)
            allowed = key_mask(start, key_block)[None]
            logits = (
                jnp.einsum(
                    "thd,shd->hts",
                    soft_query,
                    segment_attention_inputs,
                    preferred_element_type=jnp.float32,
                )
                * scale
            )
            logits = jnp.where(allowed, logits, -1e30)
            fresh = jnp.maximum(top, jnp.max(logits, axis=2))
            factor = jnp.exp(top - fresh)
            expo = jnp.where(allowed, jnp.exp(logits - fresh[:, :, None]), 0.0)
            total = total * factor + jnp.sum(expo, axis=2)
            accum = accum * factor[:, :, None] + jnp.einsum(
                "hts,shd->htd",
                expo.astype(jnp.bfloat16),
                block_values,
                preferred_element_type=jnp.float32,
            )
            return (fresh, total, accum)

        return (lax.cond(unused(start), lambda inner: inner, forward_update, carry), None)

    start_carry = (
        jnp.full((heads, tok_rows), -1e30, jnp.float32),
        jnp.zeros((heads, tok_rows), jnp.float32),
        jnp.zeros((heads, tok_rows, width), jnp.float32),
    )
    (top, total, accum), _ = lax.scan(forward_block, start_carry, block_order)
    soft_out = jnp.transpose(accum / total[:, :, None], (1, 0, 2)).astype(jnp.bfloat16)
    lse = top + jnp.log(total)
    delta = jnp.sum(soft_grads.astype(jnp.float32) * soft_out.astype(jnp.float32), axis=2).T
    all_lse, all_delta = (
        lax.all_gather(lse, "seq", axis=1, tiled=True),
        lax.all_gather(delta, "seq", axis=1, tiled=True),
    )
    zero_rows = jnp.zeros((tok_rows, heads, width), jnp.float32)

    def query_block(carry, index):
        start = index * key_block

        def query_update(inner):
            segment_attention_inputs, block_values = held_block(start)
            allowed = key_mask(start, key_block)[None]
            logits = (
                jnp.einsum(
                    "thd,shd->hts",
                    soft_query,
                    segment_attention_inputs,
                    preferred_element_type=jnp.float32,
                )
                * scale
            )
            prob = jnp.where(
                allowed, jnp.exp(jnp.where(allowed, logits - lse[:, :, None], -1e30)), 0.0
            )
            dprob = jnp.einsum(
                "thd,shd->hts", soft_grads, block_values, preferred_element_type=jnp.float32
            )
            dlogit = (prob * (dprob - delta[:, :, None])).astype(jnp.bfloat16)
            return (
                inner
                + jnp.einsum(
                    "hts,shd->thd",
                    dlogit,
                    segment_attention_inputs,
                    preferred_element_type=jnp.float32,
                )
                * scale
            )

        return (lax.cond(unused(start), lambda inner: inner, query_update, carry), None)

    soft_dq, _ = lax.scan(query_block, zero_rows, block_order)

    def key_terms(piece_query, piece_grads, start, count):
        query_pos = start + jnp.arange(count, dtype=jnp.int32)
        query_ids = lax.dynamic_slice_in_dim(all_ids, start, count)
        lse_part = lax.dynamic_slice_in_dim(all_lse, start, count, 1)
        delta_part = lax.dynamic_slice_in_dim(all_delta, start, count, 1)
        allowed = (
            (positions[None, :] <= query_pos[:, None]) & (doc_ids[None, :] == query_ids[:, None])
        )[None]
        logits = (
            jnp.einsum("thd,shd->hts", piece_query, soft_keys, preferred_element_type=jnp.float32)
            * scale
        )
        prob = jnp.where(
            allowed, jnp.exp(jnp.where(allowed, logits - lse_part[:, :, None], -1e30)), 0.0
        )
        dv_part = jnp.einsum(
            "hts,thd->shd",
            prob.astype(jnp.bfloat16),
            piece_grads,
            preferred_element_type=jnp.float32,
        )
        dprob = jnp.einsum(
            "thd,shd->hts", piece_grads, soft_values, preferred_element_type=jnp.float32
        )
        dlogit = (prob * (dprob - delta_part[:, :, None])).astype(jnp.bfloat16)
        dk_part = (
            jnp.einsum("hts,thd->shd", dlogit, piece_query, preferred_element_type=jnp.float32)
            * scale
        )
        return (dk_part, dv_part)

    def key_piece(carry, piece_query, piece_grads, start):
        count = piece_query.shape[0]
        span_rows = count
        span_count = count // span_rows

        def span_step(inner, index):
            begin = index * span_rows
            query_part = piece_query.reshape(span_rows, heads, width)
            grads_part = piece_grads.reshape(span_rows, heads, width)
            query_start = start + begin

            def span_update(sums):
                dk_part, dv_part = key_terms(query_part, grads_part, query_start, span_rows)
                return (sums[0] + dk_part, sums[1] + dv_part)

            skipped = (query_start + span_rows - 1 < offset) | (query_start > doc_end)
            return (lax.cond(skipped, lambda sums: sums, span_update, inner), None)

        result, _ = lax.scan(span_step, carry, jnp.arange(span_count, dtype=jnp.int32))
        return result

    grad_pair = key_piece((zero_rows, zero_rows), soft_q, soft_grad_out, offset)
    for step in range(1, reach + 1):
        near_query, near_grads = from_behind((soft_q, soft_grad_out), "seq", -step)
        later_start = jnp.minimum(offset + step * tok_rows, total_rows - tok_rows)
        grad_pair = key_piece(grad_pair, near_query, near_grads, later_start)
    soft_dk, soft_dv = grad_pair
    flat = (tok_rows, heads * width)
    return (
        lightning_output.reshape(flat).astype(jnp.bfloat16),
        lightning_query_gradient.reshape(flat).astype(jnp.bfloat16),
        lightning_key_gradient.reshape(flat).astype(jnp.bfloat16),
        lightning_value_gradient.reshape(flat).astype(jnp.bfloat16),
        soft_out.reshape(flat),
        soft_dq.reshape(flat).astype(jnp.bfloat16),
        soft_dk.reshape(flat).astype(jnp.bfloat16),
        soft_dv.reshape(flat).astype(jnp.bfloat16),
    )


def solution(mesh):
    return jax.shard_map(
        per_device,
        mesh=mesh,
        in_specs=(
            P(("dp", "seq")),
            P(("dp", "seq"), "head"),
            P(("dp", "seq"), "head"),
            P(("dp", "seq"), "head"),
            P("head"),
            P(("dp", "seq"), "head"),
            P(("dp", "seq"), "head"),
            P(("dp", "seq"), "head"),
            P(("dp", "seq"), "head"),
            P(("dp", "seq"), "head"),
        ),
        out_specs=(
            P(("dp", "seq"), "head"),
            P(("dp", "seq"), "head"),
            P(("dp", "seq"), "head"),
            P(("dp", "seq"), "head"),
            P(("dp", "seq"), "head"),
            P(("dp", "seq"), "head"),
            P(("dp", "seq"), "head"),
            P(("dp", "seq"), "head"),
        ),
        check_vma=False,
    )
```

profile of v0, /device:TPU:449, one launch (start us, length us, event | category | flops | bytes accessed | tf_op | source)
XLA Modules:
  0.0 608.3 jit_solution(9035415345638498831)
XLA Ops:
  19.4 23.6 %all-reduce.3 = (f32[16]{0:T(128)S(1)}, f32[16]{0:T(128)S(1)}, f32[64]{0:T(128)S(1)}) all-reduce(f32[16]{0:T(128)S(1)} %get-tuple-element.2322, f32[16]{0:T(128)S(1)} %slice_dynamic-update-slice_fusion, f32[64]{0:T(128)S(1)} %get-tuple-element.2325), channel_id=1, replica_groups=mesh['dp'=4,'seq'=16,'head'=8] {'seq'}, use_global_device_ids=true, to_apply=%add | all-reduce | flops 96 | bytes 768
  43.3 16.0 %all-gather.15.cloned.1.call-done = f32[64,128,128]{2,1,0:T(8,128)} async-done(((f32[4,128,128]{2,1,0:T(8,128)}), f32[64,128,128]{2,1,0:T(8,128)}) %all-gather.15.cloned.1.call-update) | async-done | bytes 4194320 | tf_op jit(solution)/shard_map/all_gather | solution.py:13
  62.6 8.3 %collective-permute-start.15 = (bf16[256,512]{0,1:T(8,128)(2,1)}, bf16[256,512]{0,1:T(8,128)(2,1)}, u32[]{:S(2)}, u32[]{:S(2)}) collective-permute-start(bf16[256,512]{0,1:T(8,128)(2,1)} %copy.333), channel_id=1, source_target_pairs={{8,0},{16,8},{24,16},{32,24},{40,32},{48,40},{56,48},{64,56},{72,6... | collective-permute-start | bytes 786440 | tf_op jit(solution)/shard_map/ppermute | solution.py:28
  70.9 12.9 %collective-permute-start.13 = (bf16[256,512]{0,1:T(8,128)(2,1)}, bf16[256,512]{0,1:T(8,128)(2,1)}, u32[]{:S(2)}, u32[]{:S(2)}) collective-permute-start(bf16[256,512]{0,1:T(8,128)(2,1)} %copy.333), channel_id=1, source_target_pairs={{16,0},{24,8},{32,16},{40,24},{48,32},{56,40},{64,48},{72,56},{80,... | collective-permute-start | bytes 786440 | tf_op jit(solution)/shard_map/ppermute | solution.py:28
  84.7 9.4 %collective-permute-start.14 = (bf16[256,512]{0,1:T(8,128)(2,1)}, bf16[256,512]{0,1:T(8,128)(2,1)}, u32[]{:S(2)}, u32[]{:S(2)}) collective-permute-start(bf16[256,512]{0,1:T(8,128)(2,1)} %copy.329), channel_id=1, source_target_pairs={{8,0},{16,8},{24,16},{32,24},{40,32},{48,40},{56,48},{64,56},{72,6... | collective-permute-start | bytes 786440 | tf_op jit(solution)/shard_map/ppermute | solution.py:28
  94.1 13.4 %collective-permute-start.12 = (bf16[256,512]{0,1:T(8,128)(2,1)}, bf16[256,512]{0,1:T(8,128)(2,1)}, u32[]{:S(2)}, u32[]{:S(2)}) collective-permute-start(bf16[256,512]{0,1:T(8,128)(2,1)} %copy.329), channel_id=1, source_target_pairs={{16,0},{24,8},{32,16},{40,24},{48,32},{56,40},{64,48},{72,56},{80,... | collective-permute-start | bytes 786440 | tf_op jit(solution)/shard_map/ppermute | solution.py:28
  107.4 19.6 %collective-permute-start.11 = (bf16[256,512]{0,1:T(8,128)(2,1)}, bf16[256,512]{0,1:T(8,128)(2,1)S(1)}, u32[]{:S(2)}, u32[]{:S(2)}) collective-permute-start(bf16[256,512]{0,1:T(8,128)(2,1)} %copy.333), channel_id=1, source_target_pairs={{24,0},{32,8},{40,16},{48,24},{56,32},{64,40},{72,48},{80,56},{88,... | collective-permute-start | bytes 786440 | tf_op jit(solution)/shard_map/ppermute | solution.py:28
  127.0 64.7 %all-gather.3 = s32[16,1,256]{2,1,0:T(1,128)} all-gather(s32[1,1,256]{2,1,0:T(1,128)S(1)} %bitcast.397), channel_id=1, replica_groups=mesh['dp'=4,'seq'=16,'head'=8] {'seq'}, dimensions={0}, use_global_device_ids=true | all-gather | bytes 17408 | tf_op jit(solution)/shard_map/all_gather | solution.py:88
  192.3 2.7 convert_reduce_fusion
  196.9 1.8 copy.336
  200.8 20.5 %while.47 = (s32[]{:T(128)}, f32[4,256]{1,0:T(4,128)S(1)}, f32[4,256]{1,0:T(4,128)S(1)}, f32[4,256,128]{2,1,0:T(8,128)S(1)}, s32[8]{0:T(128)S(1)}, /*index=5*/s3...) while((s32[]{:T(128)}, f32[4,256]{1,0:T(4,128)S(1)}, ...), condition=%wide.region_10.11_spmd.clone, body=%wide.region_5.10_spmd.clone.sunk | while | flops 275909376 | bytes 11353485 | solution.py:238
  216.3 4.9 conditional.31
  217.3 1.7 constant_dynamic-slice_fusion
  221.5 1.7 multiply_reduce_fusion
  225.0 6.3 %collective-permute-start.10 = (bf16[256,512]{0,1:T(8,128)(2,1)}, bf16[256,512]{0,1:T(8,128)(2,1)S(1)}, u32[]{:S(2)}, u32[]{:S(2)}) collective-permute-start(bf16[256,512]{0,1:T(8,128)(2,1)} %copy.329), channel_id=1, source_target_pairs={{24,0},{32,8},{40,16},{48,24},{56,32},{64,40},{72,48},{80,56},{88,... | collective-permute-start | bytes 786440 | tf_op jit(solution)/shard_map/ppermute | solution.py:28
  232.4 19.6 %collective-permute-start.9 = (bf16[256,512]{0,1:T(8,128)(2,1)}, bf16[256,512]{0,1:T(8,128)(2,1)}, u32[]{:S(2)}, u32[]{:S(2)}) collective-permute-start(bf16[256,512]{0,1:T(8,128)(2,1)} %copy.333), channel_id=1, source_target_pairs={{32,0},{40,8},{48,16},{56,24},{64,32},{72,40},{80,48},{88,56},{96,... | collective-permute-start | bytes 786440 | tf_op jit(solution)/shard_map/ppermute | solution.py:28
  252.0 2.0 collective-permute-start.8
  254.0 2.0 collective-permute-start.7
  256.0 2.0 collective-permute-start.6
  258.0 26.9 %collective-permute-start.5 = (bf16[256,512]{0,1:T(8,128)(2,1)}, bf16[256,512]{0,1:T(8,128)(2,1)}, u32[]{:S(2)}, u32[]{:S(2)}) collective-permute-start(bf16[256,512]{0,1:T(8,128)(2,1)} %copy.333), channel_id=1, source_target_pairs={{48,0},{56,8},{64,16},{72,24},{80,32},{88,40},{96,48},{104,56},{11... | collective-permute-start | bytes 786440 | tf_op jit(solution)/shard_map/ppermute | solution.py:28
  286.4 28.5 %while.48 = (s32[]{:T(128)}, f32[256,4,128]{0,2,1:T(8,128)}, s32[8]{0:T(128)}, s32[]{:T(128)}, s32[]{:T(128)}, /*index=5*/bf16[4096,512]{0,1:T(8,128)(2,1)}, s32...) while((s32[]{:T(128)}, f32[256,4,128]{0,2,1:T(8,128)}, ...), condition=%wide.region_15.16_spmd.clone, body=%wide.region_12.15_spmd.clone.sunk | while | flops 406979328 | bytes 9739665 | solution.py:283
  307.7 7.2 %conditional.32 = (f32[256,4,128]{0,2,1:T(8,128)}) conditional(s32[]{:T(128)} %convert_element_type.428, (s32[]{:T(128)}, bf16[4096,512]{0,1:T(8,128)(2,1)}, s32[]{:T(128)}, s32[4096]{0:T(1024)}, s32[256]{0:T(256)S(1)}, /*index=5*/bf16[256,4,128]{2,0,1:T(8,128)(2,1)S(1)}, f32[4,256]{1,0:T(4,128)}, bf16[4096,512]{0,1:T(8,128)(2,1)}, ...), branch_computations={%region_13.13_spmd, %region_14.14_spmd} | conditional | flops 406979328 | bytes 9738326 | solution.py:281
  308.7 2.5 constant_dynamic-slice_fusion.2
  311.7 3.2 fusion.23
  316.9 1.8 copy.408
  320.1 31.3 %collective-permute-start.4 = (bf16[256,512]{0,1:T(8,128)(2,1)}, bf16[256,512]{0,1:T(8,128)(2,1)}, u32[]{:S(2)}, u32[]{:S(2)}) collective-permute-start(bf16[256,512]{0,1:T(8,128)(2,1)} %copy.329), channel_id=1, source_target_pairs={{48,0},{56,8},{64,16},{72,24},{80,32},{88,40},{96,48},{104,56},{11... | collective-permute-start | bytes 786440 | tf_op jit(solution)/shard_map/ppermute | solution.py:28
  351.4 2.0 collective-permute-start.3
  353.4 2.0 collective-permute-start.2
  355.4 2.0 collective-permute-start.1
  357.4 2.0 collective-permute-start
  361.5 42.2 %all_gather.55 = f32[4,4096]{0,1:T(8,128)S(1)} all-gather(f32[4,256]{0,1:T(8,128)S(1)} %bitcast.376), channel_id=1, replica_groups=mesh['dp'=4,'seq'=16,'head'=8] {'seq'}, dimensions={1}, use_global_device_ids=true | all-gather | bytes 69632 | tf_op jit(solution)/shard_map/all_gather | solution.py:244
  403.7 22.0 %all_gather.54 = f32[4,4096]{1,0:T(4,128)} all-gather(f32[4,256]{1,0:T(4,128)S(1)} %copy-done.30), channel_id=1, replica_groups=mesh['dp'=4,'seq'=16,'head'=8] {'seq'}, dimensions={1}, use_global_device_ids=true | all-gather | bytes 69632 | tf_op jit(solution)/shard_map/all_gather | solution.py:243
  426.6 9.7 %conditional.18 = (f32[256,4,128]{2,0,1:T(8,128)S(1)}, f32[256,4,128]{2,0,1:T(8,128)S(1)}) conditional(s32[]{:T(128)} %convert_element_type.265, (s32[256]{0:T(256)S(1)}, s32[]{:T(128)}, s32[256]{0:T(256)S(1)}, s32[4096]{0:T(1024)}, bf16[256,4,128]{0,2,1:T(8,128)(2,1)}, /*index=5*/bf16[256,4,128]{0,2,1:T(8,128)(2,1)S(1)}, f32[4,4096]{1,0:T(4,128)}, ...), branch_computations={%region_17.18_spmd, %region_18.19_spmd} | conditional | flops 271122688 | bytes 10255450 | solution.py:332
  428.9 2.4 fusion.37
  432.3 2.1 fusion.42
  434.5 1.8 fusion.43
  436.3 8.6 %conditional.19 = ((f32[256,4,128]{2,0,1:T(8,128)S(1)}, f32[256,4,128]{2,0,1:T(8,128)S(1)})) conditional(s32[]{:T(128)} %convert_element_type.264, (s32[256]{0:T(256)S(1)}, s32[]{:T(128)}, s32[256]{0:T(256)S(1)}, s32[4096]{0:T(1024)}, bf16[256,4,128]{0,2,1:T(8,128)(2,1)}, /*index=5*/bf16[256,4,128]{0,2,1:T(8,128)(2,1)}, f32[4,4096]{1,0:T(4,128)}, ...), branch_computations={%region_19.20_spmd, %region_20.21_spmd} | conditional | flops 271122688 | bytes 7109702 | solution.py:332
  438.6 2.5 fusion.50
  441.1 2.1 fusion.55
  443.2 1.7 fusion.56
  444.9 8.6 %conditional.20 = ((f32[256,4,128]{2,0,1:T(8,128)S(1)}, f32[256,4,128]{2,0,1:T(8,128)S(1)})) conditional(s32[]{:T(128)} %convert_element_type.263, (s32[256]{0:T(256)S(1)}, s32[]{:T(128)}, s32[256]{0:T(256)S(1)}, s32[4096]{0:T(1024)}, bf16[256,4,128]{0,2,1:T(8,128)(2,1)}, /*index=5*/bf16[256,4,128]{0,2,1:T(8,128)(2,1)}, f32[4,4096]{1,0:T(4,128)}, ...), branch_computations={%region_21.22_spmd, %region_22.23_spmd} | conditional | flops 271122688 | bytes 7109702 | solution.py:332
  447.2 2.5 fusion.63
  449.7 2.1 fusion.68
  453.5 8.8 %conditional.21 = ((f32[256,4,128]{2,0,1:T(8,128)S(1)}, f32[256,4,128]{2,0,1:T(8,128)S(1)})) conditional(s32[]{:T(128)} %convert_element_type.262, (s32[256]{0:T(256)S(1)}, s32[]{:T(128)}, s32[256]{0:T(256)S(1)}, s32[4096]{0:T(1024)}, bf16[256,4,128]{0,2,1:T(8,128)(2,1)}, /*index=5*/bf16[256,4,128]{0,2,1:T(8,128)(2,1)}, f32[4,4096]{1,0:T(4,128)}, ...), branch_computations={%region_23.24_spmd, %region_24.25_spmd} | conditional | flops 271122688 | bytes 7109702 | solution.py:332
  456.0 2.5 fusion.76
  458.5 2.1 fusion.81
  460.6 1.7 fusion.82
  462.3 8.6 %conditional.22 = ((f32[256,4,128]{2,0,1:T(8,128)S(1)}, f32[256,4,128]{2,0,1:T(8,128)S(1)})) conditional(s32[]{:T(128)} %convert_element_type.261, (s32[256]{0:T(256)S(1)}, s32[]{:T(128)}, s32[256]{0:T(256)S(1)}, s32[4096]{0:T(1024)}, bf16[256,4,128]{0,2,1:T(8,128)(2,1)}, /*index=5*/bf16[256,4,128]{0,2,1:T(8,128)(2,1)}, f32[4,4096]{1,0:T(4,128)}, ...), branch_computations={%region_25.26_spmd, %region_26.27_spmd} | conditional | flops 271122688 | bytes 7109702 | solution.py:332
  464.6 2.5 fusion.89
  467.1 2.1 fusion.94
  470.9 8.6 %conditional.23 = ((f32[256,4,128]{2,0,1:T(8,128)S(1)}, f32[256,4,128]{2,0,1:T(8,128)S(1)})) conditional(s32[]{:T(128)} %convert_element_type.260, (s32[256]{0:T(256)S(1)}, s32[]{:T(128)}, s32[256]{0:T(256)S(1)}, s32[4096]{0:T(1024)}, bf16[256,4,128]{0,2,1:T(8,128)(2,1)}, /*index=5*/bf16[256,4,128]{0,2,1:T(8,128)(2,1)}, f32[4,4096]{1,0:T(4,128)}, ...), branch_computations={%region_27.28_spmd, %region_28.29_spmd} | conditional | flops 271122688 | bytes 7109702 | solution.py:332
  473.2 2.5 fusion.102
  475.7 2.1 fusion.107
  477.8 1.7 fusion.108
  479.5 8.6 %conditional.24 = ((f32[256,4,128]{2,0,1:T(8,128)S(1)}, f32[256,4,128]{2,0,1:T(8,128)S(1)})) conditional(s32[]{:T(128)} %convert_element_type.259, (s32[256]{0:T(256)S(1)}, s32[]{:T(128)}, s32[256]{0:T(256)S(1)}, s32[4096]{0:T(1024)}, bf16[256,4,128]{0,2,1:T(8,128)(2,1)}, /*index=5*/bf16[256,4,128]{0,2,1:T(8,128)(2,1)}, f32[4,4096]{1,0:T(4,128)}, ...), branch_computations={%region_29.30_spmd, %region_30.31_spmd} | conditional | flops 271122688 | bytes 7109702 | solution.py:332
  481.8 2.5 fusion.115
  484.3 2.1 fusion.120
  486.4 1.7 fusion.121
  488.1 8.6 %conditional.25 = ((f32[256,4,128]{2,0,1:T(8,128)S(1)}, f32[256,4,128]{2,0,1:T(8,128)S(1)})) conditional(s32[]{:T(128)} %convert_element_type.258, (s32[256]{0:T(256)S(1)}, s32[]{:T(128)}, s32[256]{0:T(256)S(1)}, s32[4096]{0:T(1024)}, bf16[256,4,128]{0,2,1:T(8,128)(2,1)}, /*index=5*/bf16[256,4,128]{0,2,1:T(8,128)(2,1)}, f32[4,4096]{1,0:T(4,128)}, ...), branch_computations={%region_31.32_spmd, %region_32.33_spmd} | conditional | flops 271122688 | bytes 7109702 | solution.py:332
  490.4 2.5 fusion.128
  492.9 2.1 fusion.133
  495.0 1.7 fusion.134
  496.8 7.6 %conditional.26 = (bf16[256,512]{1,0:T(8,128)(2,1)S(1)}, bf16[256,512]{1,0:T(8,128)(2,1)S(1)}) conditional(s32[]{:T(128)} %convert_element_type.257, (s32[256]{0:T(256)S(1)}, s32[]{:T(128)}, s32[256]{0:T(256)S(1)}, s32[4096]{0:T(1024)}, bf16[256,512]{0,1:T(8,128)(2,1)}, /*index=5*/bf16[256,4,128]{0,2,1:T(8,128)(2,1)}, f32[4,4096]{1,0:T(4,128)}, ...), branch_computations={%region_33.34_spmd, %region_34.35_spmd} | conditional | flops 271384832 | bytes 10779738
  505.1 92.7 %while.45 = (s32[]{:T(128)}, f32[4,128,128]{2,1,0:T(8,128)S(1)}, f32[]{:T(128)}, s32[]{:T(128)}, f32[16]{0:T(128)S(1)}, /*index=5*/f32[16]{0:T(128)S(1)}, f32[16...) while((s32[]{:T(128)}, f32[4,128,128]{2,1,0:T(8,128)S(1)}, ...), condition=%wide.region_1.2_spmd, body=%wide.region_0.1_spmd.sunk | while | flops 262154 | bytes 786708 | solution.py:22
  (359 shorter events, 129.6 us)
Async XLA Ops:
  7.2 53.5 %copy-start = (bf16[256,512]{1,0:T(8,128)(2,1)S(1)}, bf16[256,512]{1,0:T(8,128)(2,1)}, u32[]{:S(2)}) copy-start(bf16[256,512]{1,0:T(8,128)(2,1)} %param.43) | copy-start | bytes 786436
  7.2 12.1 %copy-start.32 = (f32[4]{0:T(128)S(1)}, f32[4]{0:T(128)}, u32[]{:S(2)}) copy-start(f32[4]{0:T(128)} %param.44) | copy-start | bytes 52
  7.2 8.8 %copy-start.22 = (bf16[256,512]{1,0:T(8,128)(2,1)S(1)}, bf16[256,512]{1,0:T(8,128)(2,1)}, u32[]{:S(2)}) copy-start(bf16[256,512]{1,0:T(8,128)(2,1)} %param.48) | copy-start | bytes 786436
  7.2 9.8 %copy-start.23 = (bf16[256,512]{1,0:T(8,128)(2,1)S(1)}, bf16[256,512]{1,0:T(8,128)(2,1)}, u32[]{:S(2)}) copy-start(bf16[256,512]{1,0:T(8,128)(2,1)} %param.47) | copy-start | bytes 786436
  7.2 35.9 %copy-start.12 = (bf16[256,512]{1,0:T(8,128)(2,1)S(1)}, bf16[256,512]{1,0:T(8,128)(2,1)}, u32[]{:S(2)}) copy-start(bf16[256,512]{1,0:T(8,128)(2,1)} %param.42) | copy-start | bytes 786436
  7.2 52.0 %all-gather.15.cloned.1.call-start = ((), (), s32[]{:S(2)}) async-start(), calls=%async_computation.3 | async-start | bytes 4456448 | tf_op jit(solution)/shard_map/all_gather | solution.py:13
  7.3 35.9 %copy-start.34 = (f32[256]{0:T(256)}, f32[256]{0:T(256)S(1)}, u32[]{:S(2)}) copy-start(f32[256]{0:T(256)S(1)} %convert_negate_fusion) | copy-start | bytes 3076
  13.0 218.3 %copy-start.7 = (bf16[256,512]{0,1:T(8,128)(2,1)}, bf16[256,512]{0,1:T(8,128)(2,1)S(1)}, u32[]{:S(2)}) copy-start(bf16[256,512]{0,1:T(8,128)(2,1)S(1)} %copy.484) | copy-start | bytes 786436
  14.2 184.7 %copy-start.9 = (bf16[256,512]{0,1:T(8,128)(2,1)}, bf16[256,512]{0,1:T(8,128)(2,1)S(1)}, u32[]{:S(2)}) copy-start(bf16[256,512]{0,1:T(8,128)(2,1)S(1)} %copy.485) | copy-start | bytes 786436
  16.0 184.7 %all-gather.11.cloned.1.call-start = ((), (), s32[]{:S(2)}) async-start(), calls=%async_computation.1 | async-start | bytes 4456448 | tf_op jit(solution)/shard_map/all_gather | solution.py:177
  16.9 183.8 %all-gather.9.cloned.1.call-start = ((), (), s32[]{:S(2)}) async-start(), calls=%async_computation | async-start | bytes 4456448 | tf_op jit(solution)/shard_map/all_gather | solution.py:176
  17.8 486.5 %all-gather.13.cloned.1.call-start = ((), (), s32[]{:S(2)}) async-start(), calls=%async_computation.2 | async-start | bytes 4456448 | tf_op jit(solution)/shard_map/all_gather | solution.py:13
  43.2 17.5 %copy-start.13 = (bf16[256,512]{0,1:T(8,128)(2,1)}, bf16[256,512]{0,1:T(8,128)(2,1)S(1)}, u32[]{:S(2)}) copy-start(bf16[256,512]{0,1:T(8,128)(2,1)S(1)} %copy.512) | copy-start | bytes 786436
  59.3 0.7 copy-start.21
  59.3 2.4 copy-start.24
  59.3 24.5 %copy-start.25 = (bf16[256,512]{1,0:T(8,128)(2,1)S(1)}, bf16[256,512]{1,0:T(8,128)(2,1)}, u32[]{:S(2)}) copy-start(bf16[256,512]{1,0:T(8,128)(2,1)} %param.46) | copy-start | bytes 786436
  59.3 0.5 copy-start.36
  59.4 34.7 %copy-start.31 = (f32[16,4]{1,0:T(8,128)}, f32[16,4]{1,0:T(8,128)S(1)}, u32[]{:S(2)}) copy-start(f32[16,4]{1,0:T(8,128)S(1)} %get-tuple-element.2858) | copy-start | bytes 772
  59.4 139.9 %copy-start.38 = (f32[16]{0:T(128)}, f32[16]{0:T(128)S(1)}, u32[]{:S(2)}) copy-start(f32[16]{0:T(128)S(1)} %get-tuple-element.2860) | copy-start | bytes 196
  62.6 162.4 %collective-permute-start.15 = (bf16[256,512]{0,1:T(8,128)(2,1)}, bf16[256,512]{0,1:T(8,128)(2,1)}, u32[]{:S(2)}, u32[]{:S(2)}) collective-permute-start(bf16[256,512]{0,1:T(8,128)(2,1)} %copy.333), channel_id=1, source_target_pairs={{8,0},{16,8},{24,16},{32,24},{40,32},{48,40},{56,48},{64,56},{72,6... | collective-permute-start | bytes 786440 | tf_op jit(solution)/shard_map/ppermute | solution.py:28
  70.9 181.1 %collective-permute-start.13 = (bf16[256,512]{0,1:T(8,128)(2,1)}, bf16[256,512]{0,1:T(8,128)(2,1)}, u32[]{:S(2)}, u32[]{:S(2)}) collective-permute-start(bf16[256,512]{0,1:T(8,128)(2,1)} %copy.333), channel_id=1, source_target_pairs={{16,0},{24,8},{32,16},{40,24},{48,32},{56,40},{64,48},{72,56},{80,... | collective-permute-start | bytes 786440 | tf_op jit(solution)/shard_map/ppermute | solution.py:28
  84.7 147.7 %collective-permute-start.14 = (bf16[256,512]{0,1:T(8,128)(2,1)}, bf16[256,512]{0,1:T(8,128)(2,1)}, u32[]{:S(2)}, u32[]{:S(2)}) collective-permute-start(bf16[256,512]{0,1:T(8,128)(2,1)} %copy.329), channel_id=1, source_target_pairs={{8,0},{16,8},{24,16},{32,24},{40,32},{48,40},{56,48},{64,56},{72,6... | collective-permute-start | bytes 786440 | tf_op jit(solution)/shard_map/ppermute | solution.py:28
  94.1 160.0 %collective-permute-start.12 = (bf16[256,512]{0,1:T(8,128)(2,1)}, bf16[256,512]{0,1:T(8,128)(2,1)}, u32[]{:S(2)}, u32[]{:S(2)}) collective-permute-start(bf16[256,512]{0,1:T(8,128)(2,1)} %copy.329), channel_id=1, source_target_pairs={{16,0},{24,8},{32,16},{40,24},{48,32},{56,40},{64,48},{72,56},{80,... | collective-permute-start | bytes 786440 | tf_op jit(solution)/shard_map/ppermute | solution.py:28
  107.4 148.6 %collective-permute-start.11 = (bf16[256,512]{0,1:T(8,128)(2,1)}, bf16[256,512]{0,1:T(8,128)(2,1)S(1)}, u32[]{:S(2)}, u32[]{:S(2)}) collective-permute-start(bf16[256,512]{0,1:T(8,128)(2,1)} %copy.333), channel_id=1, source_target_pairs={{24,0},{32,8},{40,16},{48,24},{56,32},{64,40},{72,48},{80,56},{88,... | collective-permute-start | bytes 786440 | tf_op jit(solution)/shard_map/ppermute | solution.py:28
  199.3 32.0 %copy-start.5 = (f32[4,256,256]{2,1,0:T(8,128)}, f32[4,256,256]{2,1,0:T(8,128)S(1)}, u32[]{:S(2)}) copy-start(f32[4,256,256]{2,1,0:T(8,128)S(1)} %convolution_multiply_fusion.9) | copy-start | bytes 3145732
  224.0 62.4 %copy-start.16 = (f32[256,4]{1,0:T(8,128)}, f32[256,4]{1,0:T(8,128)S(1)}, u32[]{:S(2)}) copy-start(f32[256,4]{1,0:T(8,128)S(1)} %copy.482) | copy-start | bytes 12292
  225.0 33.0 %collective-permute-start.10 = (bf16[256,512]{0,1:T(8,128)(2,1)}, bf16[256,512]{0,1:T(8,128)(2,1)S(1)}, u32[]{:S(2)}, u32[]{:S(2)}) collective-permute-start(bf16[256,512]{0,1:T(8,128)(2,1)} %copy.329), channel_id=1, source_target_pairs={{24,0},{32,8},{40,16},{48,24},{56,32},{64,40},{72,48},{80,56},{88,... | collective-permute-start | bytes 786440 | tf_op jit(solution)/shard_map/ppermute | solution.py:28
  232.4 87.7 %collective-permute-start.9 = (bf16[256,512]{0,1:T(8,128)(2,1)}, bf16[256,512]{0,1:T(8,128)(2,1)}, u32[]{:S(2)}, u32[]{:S(2)}) collective-permute-start(bf16[256,512]{0,1:T(8,128)(2,1)} %copy.333), channel_id=1, source_target_pairs={{32,0},{40,8},{48,16},{56,24},{64,32},{72,40},{80,48},{88,56},{96,... | collective-permute-start | bytes 786440 | tf_op jit(solution)/shard_map/ppermute | solution.py:28
  252.0 99.4 %collective-permute-start.8 = (bf16[256,512]{0,1:T(8,128)(2,1)}, bf16[256,512]{0,1:T(8,128)(2,1)}, u32[]{:S(2)}, u32[]{:S(2)}) collective-permute-start(bf16[256,512]{0,1:T(8,128)(2,1)} %copy.329), channel_id=1, source_target_pairs={{32,0},{40,8},{48,16},{56,24},{64,32},{72,40},{80,48},{88,56},{96,... | collective-permute-start | bytes 786440 | tf_op jit(solution)/shard_map/ppermute | solution.py:28
  254.0 99.4 %collective-permute-start.7 = (bf16[256,512]{0,1:T(8,128)(2,1)}, bf16[256,512]{0,1:T(8,128)(2,1)}, u32[]{:S(2)}, u32[]{:S(2)}) collective-permute-start(bf16[256,512]{0,1:T(8,128)(2,1)} %copy.333), channel_id=1, source_target_pairs={{40,0},{48,8},{56,16},{64,24},{72,32},{80,40},{88,48},{96,56},{104... | collective-permute-start | bytes 786440 | tf_op jit(solution)/shard_map/ppermute | solution.py:28
  256.0 30.3 %copy-start.20 = (bf16[256,512]{0,1:T(8,128)(2,1)}, bf16[256,512]{0,1:T(8,128)(2,1)S(1)}, u32[]{:S(2)}) copy-start(bf16[256,512]{0,1:T(8,128)(2,1)S(1)} %collective-permute-done.11) | copy-start | bytes 786436
  256.0 99.4 %collective-permute-start.6 = (bf16[256,512]{0,1:T(8,128)(2,1)}, bf16[256,512]{0,1:T(8,128)(2,1)}, u32[]{:S(2)}, u32[]{:S(2)}) collective-permute-start(bf16[256,512]{0,1:T(8,128)(2,1)} %copy.329), channel_id=1, source_target_pairs={{40,0},{48,8},{56,16},{64,24},{72,32},{80,40},{88,48},{96,56},{104... | collective-permute-start | bytes 786440 | tf_op jit(solution)/shard_map/ppermute | solution.py:28
  258.0 28.3 %copy-start.28 = (bf16[256,512]{0,1:T(8,128)(2,1)}, bf16[256,512]{0,1:T(8,128)(2,1)S(1)}, u32[]{:S(2)}) copy-start(bf16[256,512]{0,1:T(8,128)(2,1)S(1)} %collective-permute-done.10) | copy-start | bytes 786436
  258.0 99.4 %collective-permute-start.5 = (bf16[256,512]{0,1:T(8,128)(2,1)}, bf16[256,512]{0,1:T(8,128)(2,1)}, u32[]{:S(2)}, u32[]{:S(2)}) collective-permute-start(bf16[256,512]{0,1:T(8,128)(2,1)} %copy.333), channel_id=1, source_target_pairs={{48,0},{56,8},{64,16},{72,24},{80,32},{88,40},{96,48},{104,56},{11... | collective-permute-start | bytes 786440 | tf_op jit(solution)/shard_map/ppermute | solution.py:28
  308.7 3.0 copy-start.29
  314.9 44.5 %copy-start.3 = (f32[4,256,256]{2,1,0:T(8,128)S(1)}, f32[4,256,256]{2,1,0:T(8,128)}, u32[]{:S(2)}) copy-start(f32[4,256,256]{2,1,0:T(8,128)} %convolution_multiply_fusion.10) | copy-start | bytes 3145732
  314.9 44.5 %copy-start.10 = (bf16[256,512]{0,1:T(8,128)(2,1)S(1)}, bf16[256,512]{0,1:T(8,128)(2,1)}, u32[]{:S(2)}) copy-start(bf16[256,512]{0,1:T(8,128)(2,1)} %copy-done.9) | copy-start | bytes 786436
  316.9 43.7 %copy-start.19 = (bf16[4,256,128]{1,2,0:T(8,128)(2,1)S(1)}, bf16[4,256,128]{1,2,0:T(8,128)(2,1)}, u32[]{:S(2)}) copy-start(bf16[4,256,128]{1,2,0:T(8,128)(2,1)} %get-tuple-element.2290) | copy-start | bytes 786436
  318.8 42.7 %copy-start.17 = (f32[256,4]{1,0:T(8,128)S(1)}, f32[256,4]{1,0:T(8,128)}, u32[]{:S(2)}) copy-start(f32[256,4]{1,0:T(8,128)} %copy-done.16) | copy-start | bytes 12292
  320.1 159.4 %collective-permute-start.4 = (bf16[256,512]{0,1:T(8,128)(2,1)}, bf16[256,512]{0,1:T(8,128)(2,1)}, u32[]{:S(2)}, u32[]{:S(2)}) collective-permute-start(bf16[256,512]{0,1:T(8,128)(2,1)} %copy.329), channel_id=1, source_target_pairs={{48,0},{56,8},{64,16},{72,24},{80,32},{88,40},{96,48},{104,56},{11... | collective-permute-start | bytes 786440 | tf_op jit(solution)/shard_map/ppermute | solution.py:28
  351.4 136.7 %collective-permute-start.3 = (bf16[256,512]{0,1:T(8,128)(2,1)}, bf16[256,512]{0,1:T(8,128)(2,1)}, u32[]{:S(2)}, u32[]{:S(2)}) collective-permute-start(bf16[256,512]{0,1:T(8,128)(2,1)} %copy.333), channel_id=1, source_target_pairs={{56,0},{64,8},{72,16},{80,24},{88,32},{96,40},{104,48},{112,56},{1... | collective-permute-start | bytes 786440 | tf_op jit(solution)/shard_map/ppermute | solution.py:28
  353.4 134.7 %collective-permute-start.2 = (bf16[256,512]{0,1:T(8,128)(2,1)}, bf16[256,512]{0,1:T(8,128)(2,1)}, u32[]{:S(2)}, u32[]{:S(2)}) collective-permute-start(bf16[256,512]{0,1:T(8,128)(2,1)} %copy.329), channel_id=1, source_target_pairs={{56,0},{64,8},{72,16},{80,24},{88,32},{96,40},{104,48},{112,56},{1... | collective-permute-start | bytes 786440 | tf_op jit(solution)/shard_map/ppermute | solution.py:28
  355.4 141.3 %collective-permute-start.1 = (bf16[256,512]{0,1:T(8,128)(2,1)}, bf16[256,512]{0,1:T(8,128)(2,1)}, u32[]{:S(2)}, u32[]{:S(2)}) collective-permute-start(bf16[256,512]{0,1:T(8,128)(2,1)} %copy.333), channel_id=1, source_target_pairs={{64,0},{72,8},{80,16},{88,24},{96,32},{104,40},{112,48},{120,56},{... | collective-permute-start | bytes 786440 | tf_op jit(solution)/shard_map/ppermute | solution.py:28
  357.4 139.3 %collective-permute-start = (bf16[256,512]{0,1:T(8,128)(2,1)}, bf16[256,512]{0,1:T(8,128)(2,1)}, u32[]{:S(2)}, u32[]{:S(2)}) collective-permute-start(bf16[256,512]{0,1:T(8,128)(2,1)} %copy.329), channel_id=1, source_target_pairs={{64,0},{72,8},{80,16},{88,24},{96,32},{104,40},{112,48},{120,56},{... | collective-permute-start | bytes 786440 | tf_op jit(solution)/shard_map/ppermute | solution.py:28
  359.8 44.0 %copy-start.30 = (f32[4,256]{1,0:T(4,128)S(1)}, f32[4,256]{1,0:T(4,128)}, u32[]{:S(2)}) copy-start(f32[4,256]{1,0:T(4,128)} %get-tuple-element.2857) | copy-start | bytes 12292
  359.8 66.8 %copy-start.1 = (bf16[256,512]{0,1:T(8,128)(2,1)S(1)}, bf16[256,512]{0,1:T(8,128)(2,1)}, u32[]{:S(2)}) copy-start(bf16[256,512]{0,1:T(8,128)(2,1)} %copy.330) | copy-start | bytes 786436
  359.8 66.8 %copy-start.18 = (bf16[256,512]{0,1:T(8,128)(2,1)S(1)}, bf16[256,512]{0,1:T(8,128)(2,1)}, u32[]{:S(2)}) copy-start(bf16[256,512]{0,1:T(8,128)(2,1)} %copy.328) | copy-start | bytes 786436
  427.5 3.8 copy-start.15
  496.7 7.7 %copy-start.37 = (f32[16]{0:T(128)S(1)}, f32[16]{0:T(128)}, u32[]{:S(2)}) copy-start(f32[16]{0:T(128)} %copy-done.36) | copy-start | bytes 196
  496.7 7.7 %copy-start.39 = (f32[16]{0:T(128)S(1)}, f32[16]{0:T(128)}, u32[]{:S(2)}) copy-start(f32[16]{0:T(128)} %copy-done.38) | copy-start | bytes 196
  498.3 2.5 copy-start.2
  504.3 0.7 copy-start.26
  504.4 0.8 copy-start.27
  504.4 93.4 %copy-start.33 = (f32[4]{0:T(128)S(1)}, f32[4]{0:T(128)}, u32[]{:S(2)}) copy-start(f32[4]{0:T(128)} %param.44) | copy-start | bytes 52
  504.5 93.4 %copy-start.35 = (f32[256]{0:T(256)S(1)}, f32[256]{0:T(256)}, u32[]{:S(2)}) copy-start(f32[256]{0:T(256)} %copy-done.34) | copy-start | bytes 3076
  504.5 93.5 %copy-start.11 = (bf16[256,512]{0,1:T(8,128)(2,1)S(1)}, bf16[256,512]{0,1:T(8,128)(2,1)}, u32[]{:S(2)}) copy-start(bf16[256,512]{0,1:T(8,128)(2,1)} %copy-done.9) | copy-start | bytes 786436
  504.5 93.9 %copy-start.8 = (bf16[256,512]{0,1:T(8,128)(2,1)S(1)}, bf16[256,512]{0,1:T(8,128)(2,1)}, u32[]{:S(2)}) copy-start(bf16[256,512]{0,1:T(8,128)(2,1)} %copy-done.7) | copy-start | bytes 786436
  597.8 1.2 copy-start.6
  597.9 1.3 copy-start.14
  598.4 2.1 copy-start.4
Sparse Core Ops, SparseCore 0:
  16.1 43.1 all-gather.14
  61.3 50.4 all-gather.10
  114.4 61.8 all-gather.8
  178.9 45.5 all-gather.12
where the time goes:
time: 613 us; the launch traced here: 608 us
  starting transfers between devices  162 us (26%)
  blocking collectives  152 us (25%)
  local copies, waits for them, and re-layouts  94.5 us (15%)
  loops' own time  70.5 us (12%)
  matrix products  68.5 us (11%)
  other arithmetic  28.5 us (5%)
  waiting for transfers between devices  16.1 us (3%)
  between operations  16 us (3%)
    ppermute x16, starting transfers between devices, from_behind(): lax.ppermute(value, axis, [(source, source + steps) for source in range(f...  162 us
    all_gather x1, blocking collectives, per_device(): all_ids = lax.all_gather(doc_ids, 'seq', axis=0, tiled=True)  64.7 us
    another operation x2, loops' own time, entering(): return lax.fori_loop(0, ahead, one, state)  47.9 us
    all_gather x1, blocking collectives, per_device(): lax.all_gather(delta, 'seq', axis=1, tiled=True)  42.2 us
    unnamed x1, blocking collectives  23.6 us
    all_gather x1, blocking collectives, per_device(): lax.all_gather(lse, 'seq', axis=1, tiled=True)  22 us
    dot_general x9, matrix products, key_terms(): jnp.einsum('thd,shd->hts', piece_query, soft_keys, preferred_element_type...  21.4 us
    dynamic_slice x30, local copies, waits for them, and re-layouts, one(): lax.dynamic_index_in_dim(a, source, 0, False)  18.4 us
  transfers between devices with their start and end apart: 20, of which 1 were waited for; matrix products, arithmetic and copies ran while one was open for 22% of the time, Pallas kernels for 0%

commit v1 on v0

--- a/solution.py
+++ b/solution.py
@@ -85,7 +85,10 @@
     total_rows = tok_rows * shards
     offset = lax.axis_index("seq") * tok_rows
     last_pos = offset + tok_rows - 1
-    all_ids = lax.all_gather(doc_ids, "seq", axis=0, tiled=True)
+    all_ids = jnp.concatenate(
+        lax.all_to_all(jnp.stack([doc_ids for _ in range(lax.axis_size("seq"))]), "seq", 0, 0),
+        axis=0,
+    )
     positions = offset + jnp.arange(tok_rows, dtype=jnp.int32)
     own_ids = doc_ids.astype(jnp.float32)
     within_segment_position = jnp.arange(tok_rows, dtype=jnp.int32)

time: 613 us -> 591 us (0.964)
  blocking collectives: 152 us -> 90.6 us
  starting transfers between devices: 162 us -> 191 us
  waiting for transfers between devices: 16.1 us -> 26.5 us
    all_gather x1 -> x0, blocking collectives: 64.7 us -> none  [per_device(): all_ids = lax.all_gather(doc_ids, 'seq', axis=0, tiled=True)]
    all_to_all x0 -> x1, starting transfers between devices: none -> 38.6 us  [per_device(): lax.all_to_all(jnp.stack([doc_ids for _ in range(lax.axis_size('seq'))]),...]
    all_to_all x0 -> x1, waiting for transfers between devices: none -> 10.3 us  [per_device(): lax.all_to_all(jnp.stack([doc_ids for _ in range(lax.axis_size('seq'))]),...]
    ppermute x16, starting transfers between devices: 162 us -> 152 us  [from_behind(): lax.ppermute(value, axis, [(source, source + steps) for source in range(f...]
  transfers between devices with their start and end apart: 20 -> 21, of which waited for: 1 -> 2; matrix products, arithmetic and copies ran while one was open for 22% -> 23% of each run, Pallas kernels for 0% -> 0%
where the time goes in v1:
time: 591 us; the launch traced here: 586 us
  starting transfers between devices  191 us (32%)
  local copies, waits for them, and re-layouts  94.7 us (16%)
  blocking collectives  90.6 us (15%)
  loops' own time  70.4 us (12%)
  matrix products  68.6 us (12%)
  other arithmetic  28.4 us (5%)
  waiting for transfers between devices  26.5 us (4%)
  between operations  16 us (3%)
    ppermute x16, starting transfers between devices, from_behind(): lax.ppermute(value, axis, [(source, source + steps) for source in range(f...  152 us
    another operation x2, loops' own time, entering(): return lax.fori_loop(0, ahead, one, state)  48.1 us
    all_gather x1, blocking collectives, per_device(): lax.all_gather(delta, 'seq', axis=1, tiled=True)  46.9 us
    all_to_all x1, starting transfers between devices, per_device(): lax.all_to_all(jnp.stack([doc_ids for _ in range(lax.axis_size('seq'))]),...  38.6 us
    unnamed x1, blocking collectives  23.6 us
    dot_general x9, matrix products, key_terms(): jnp.einsum('thd,shd->hts', piece_query, soft_keys, preferred_element_type...  21.5 us
    all_gather x1, blocking collectives, per_device(): lax.all_gather(lse, 'seq', axis=1, tiled=True)  20 us
    dot_general x9, matrix products, key_terms(): jnp.einsum('hts,thd->shd', dlogit, piece_query, preferred_element_type=jn...  18.4 us
  transfers between devices with their start and end apart: 21, of which 2 were waited for; matrix products, arithmetic and copies ran while one was open for 23% of the time, Pallas kernels for 0%

profile of v1, /device:TPU:449, one launch (start us, length us, event | category | flops | bytes accessed | tf_op | source)
XLA Modules:
  0.0 585.8 jit_solution(12118323124451201223)
XLA Ops:
  19.4 23.6 %all-reduce.3 = (f32[16]{0:T(128)S(1)}, f32[16]{0:T(128)S(1)}, f32[64]{0:T(128)S(1)}) all-reduce(f32[16]{0:T(128)S(1)} %get-tuple-element.2754, f32[16]{0:T(128)S(1)} %slice_dynamic-update-slice_fusion, f32[64]{0:T(128)S(1)} %get-tuple-element.2757), channel_id=1, replica_groups=mesh['dp'=4,'seq'=16,'head'=8] {'seq'}, use_global_device_ids=true, to_apply=%add | all-reduce | flops 96 | bytes 768
  43.2 16.0 %all-gather.14.cloned.1.call-done = f32[64,128,128]{2,1,0:T(8,128)} async-done(((f32[4,128,128]{2,1,0:T(8,128)}), f32[64,128,128]{2,1,0:T(8,128)}) %all-gather.14.cloned.1.call-update) | async-done | bytes 4194320 | tf_op jit(solution)/shard_map/all_gather | solution.py:13
  62.6 8.4 %collective-permute-start.15 = (bf16[256,512]{0,1:T(8,128)(2,1)}, bf16[256,512]{0,1:T(8,128)(2,1)}, u32[]{:S(2)}, u32[]{:S(2)}) collective-permute-start(bf16[256,512]{0,1:T(8,128)(2,1)} %copy.720), channel_id=1, source_target_pairs={{8,0},{16,8},{24,16},{32,24},{40,32},{48,40},{56,48},{64,56},{72,6... | collective-permute-start | bytes 786440 | tf_op jit(solution)/shard_map/ppermute | solution.py:28
  71.0 13.0 %collective-permute-start.13 = (bf16[256,512]{0,1:T(8,128)(2,1)}, bf16[256,512]{0,1:T(8,128)(2,1)}, u32[]{:S(2)}, u32[]{:S(2)}) collective-permute-start(bf16[256,512]{0,1:T(8,128)(2,1)} %copy.720), channel_id=1, source_target_pairs={{16,0},{24,8},{32,16},{40,24},{48,32},{56,40},{64,48},{72,56},{80,... | collective-permute-start | bytes 786440 | tf_op jit(solution)/shard_map/ppermute | solution.py:28
  84.8 9.4 %collective-permute-start.14 = (bf16[256,512]{0,1:T(8,128)(2,1)}, bf16[256,512]{0,1:T(8,128)(2,1)}, u32[]{:S(2)}, u32[]{:S(2)}) collective-permute-start(bf16[256,512]{0,1:T(8,128)(2,1)} %copy.716), channel_id=1, source_target_pairs={{8,0},{16,8},{24,16},{32,24},{40,32},{48,40},{56,48},{64,56},{72,6... | collective-permute-start | bytes 786440 | tf_op jit(solution)/shard_map/ppermute | solution.py:28
  94.1 13.4 %collective-permute-start.12 = (bf16[256,512]{0,1:T(8,128)(2,1)}, bf16[256,512]{0,1:T(8,128)(2,1)}, u32[]{:S(2)}, u32[]{:S(2)}) collective-permute-start(bf16[256,512]{0,1:T(8,128)(2,1)} %copy.716), channel_id=1, source_target_pairs={{16,0},{24,8},{32,16},{40,24},{48,32},{56,40},{64,48},{72,56},{80,... | collective-permute-start | bytes 786440 | tf_op jit(solution)/shard_map/ppermute | solution.py:28
  107.5 19.6 %collective-permute-start.11 = (bf16[256,512]{0,1:T(8,128)(2,1)}, bf16[256,512]{0,1:T(8,128)(2,1)S(1)}, u32[]{:S(2)}, u32[]{:S(2)}) collective-permute-start(bf16[256,512]{0,1:T(8,128)(2,1)} %copy.720), channel_id=1, source_target_pairs={{24,0},{32,8},{40,16},{48,24},{56,32},{64,40},{72,48},{80,56},{88,... | collective-permute-start | bytes 786440 | tf_op jit(solution)/shard_map/ppermute | solution.py:28
  127.7 38.6 %all-to-all-start = ((s32[16,1,256]{2,1,0:T(1,128)}), s32[16,1,256]{2,1,0:T(1,128)}, u32[]{:S(2)}, u32[]{:S(2)}) async-start(s32[16,1,256]{2,1,0:T(1,128)} %stack.2), calls=%async_computation | async-start | bytes 32768 | tf_op jit(solution)/shard_map/all_to_all | solution.py:89
  170.1 1.8 copy.723
  171.9 10.3 %all-to-all-done = s32[16,1,256]{2,1,0:T(1,128)} async-done(((s32[16,1,256]{2,1,0:T(1,128)}), s32[16,1,256]{2,1,0:T(1,128)}, u32[]{:S(2)}, u32[]{:S(2)}) %all-to-all-start) | async-done | bytes 16416 | tf_op jit(solution)/shard_map/all_to_all | solution.py:89
  182.2 2.7 convert_reduce_fusion
  185.7 20.5 %while.47 = (s32[]{:T(128)}, f32[4,256]{1,0:T(4,128)S(1)}, f32[4,256]{1,0:T(4,128)S(1)}, f32[4,256,128]{2,1,0:T(8,128)S(1)}, s32[8]{0:T(128)S(1)}, /*index=5*/s3...) while((s32[]{:T(128)}, f32[4,256]{1,0:T(4,128)S(1)}, ...), condition=%wide.region_10.11_spmd.clone, body=%wide.region_5.10_spmd.clone.sunk | while | flops 275909376 | bytes 11353485 | solution.py:241
  201.2 4.9 conditional.31
  202.2 1.7 constant_dynamic-slice_fusion
  206.4 1.7 multiply_reduce_fusion
  209.9 5.9 %collective-permute-start.10 = (bf16[256,512]{0,1:T(8,128)(2,1)}, bf16[256,512]{0,1:T(8,128)(2,1)S(1)}, u32[]{:S(2)}, u32[]{:S(2)}) collective-permute-start(bf16[256,512]{0,1:T(8,128)(2,1)} %copy.716), channel_id=1, source_target_pairs={{24,0},{32,8},{40,16},{48,24},{56,32},{64,40},{72,48},{80,56},{88,... | collective-permute-start | bytes 786440 | tf_op jit(solution)/shard_map/ppermute | solution.py:28
  216.9 12.0 %collective-permute-start.9 = (bf16[256,512]{0,1:T(8,128)(2,1)}, bf16[256,512]{0,1:T(8,128)(2,1)}, u32[]{:S(2)}, u32[]{:S(2)}) collective-permute-start(bf16[256,512]{0,1:T(8,128)(2,1)} %copy.720), channel_id=1, source_target_pairs={{32,0},{40,8},{48,16},{56,24},{64,32},{72,40},{80,48},{88,56},{96,... | collective-permute-start | bytes 786440 | tf_op jit(solution)/shard_map/ppermute | solution.py:28
  228.9 2.0 collective-permute-start.8
  230.9 2.0 collective-permute-start.7
  232.9 2.0 collective-permute-start.6
  234.9 25.1 %collective-permute-start.5 = (bf16[256,512]{0,1:T(8,128)(2,1)}, bf16[256,512]{0,1:T(8,128)(2,1)}, u32[]{:S(2)}, u32[]{:S(2)}) collective-permute-start(bf16[256,512]{0,1:T(8,128)(2,1)} %copy.720), channel_id=1, source_target_pairs={{48,0},{56,8},{64,16},{72,24},{80,32},{88,40},{96,48},{104,56},{11... | collective-permute-start | bytes 786440 | tf_op jit(solution)/shard_map/ppermute | solution.py:28
  261.4 27.9 %while.48 = (s32[]{:T(128)}, f32[256,4,128]{0,2,1:T(8,128)}, s32[8]{0:T(128)}, s32[]{:T(128)}, s32[]{:T(128)}, /*index=5*/bf16[4096,512]{0,1:T(8,128)(2,1)}, s32...) while((s32[]{:T(128)}, f32[256,4,128]{0,2,1:T(8,128)}, ...), condition=%wide.region_15.16_spmd.clone, body=%wide.region_12.15_spmd.clone.sunk | while | flops 406979328 | bytes 9739665 | solution.py:286
  282.1 7.2 %conditional.32 = (f32[256,4,128]{0,2,1:T(8,128)}) conditional(s32[]{:T(128)} %convert_element_type.432, (s32[]{:T(128)}, bf16[4096,512]{0,1:T(8,128)(2,1)}, s32[]{:T(128)}, s32[4096]{0:T(1024)}, s32[256]{0:T(256)S(1)}, /*index=5*/bf16[256,4,128]{2,0,1:T(8,128)(2,1)S(1)}, f32[4,256]{1,0:T(4,128)}, bf16[4096,512]{0,1:T(8,128)(2,1)}, ...), branch_computations={%region_13.13_spmd, %region_14.14_spmd} | conditional | flops 406979328 | bytes 9738326 | solution.py:284
  283.1 2.5 constant_dynamic-slice_fusion.2
  286.1 3.2 fusion.23
  291.3 1.8 copy.796
  294.5 31.2 %collective-permute-start.4 = (bf16[256,512]{0,1:T(8,128)(2,1)}, bf16[256,512]{0,1:T(8,128)(2,1)}, u32[]{:S(2)}, u32[]{:S(2)}) collective-permute-start(bf16[256,512]{0,1:T(8,128)(2,1)} %copy.716), channel_id=1, source_target_pairs={{48,0},{56,8},{64,16},{72,24},{80,32},{88,40},{96,48},{104,56},{11... | collective-permute-start | bytes 786440 | tf_op jit(solution)/shard_map/ppermute | solution.py:28
  325.8 2.0 collective-permute-start.3
  327.7 2.0 collective-permute-start.2
  329.7 2.0 collective-permute-start.1
  331.7 2.0 collective-permute-start
  335.8 46.9 %all_gather.51 = f32[4,4096]{0,1:T(8,128)S(1)} all-gather(f32[4,256]{0,1:T(8,128)S(1)} %bitcast.375), channel_id=1, replica_groups=mesh['dp'=4,'seq'=16,'head'=8] {'seq'}, dimensions={1}, use_global_device_ids=true | all-gather | bytes 69632 | tf_op jit(solution)/shard_map/all_gather | solution.py:247
  382.7 20.0 %all_gather.50 = f32[4,4096]{1,0:T(4,128)} all-gather(f32[4,256]{1,0:T(4,128)S(1)} %copy-done.30), channel_id=1, replica_groups=mesh['dp'=4,'seq'=16,'head'=8] {'seq'}, dimensions={1}, use_global_device_ids=true | all-gather | bytes 69632 | tf_op jit(solution)/shard_map/all_gather | solution.py:246
  403.7 9.7 %conditional.18 = (f32[256,4,128]{2,0,1:T(8,128)S(1)}, f32[256,4,128]{2,0,1:T(8,128)S(1)}) conditional(s32[]{:T(128)} %convert_element_type.269, (s32[256]{0:T(256)S(1)}, s32[]{:T(128)}, s32[256]{0:T(256)S(1)}, s32[4096]{0:T(1024)}, bf16[256,4,128]{0,2,1:T(8,128)(2,1)}, /*index=5*/bf16[256,4,128]{0,2,1:T(8,128)(2,1)S(1)}, f32[4,4096]{1,0:T(4,128)}, ...), branch_computations={%region_17.18_spmd, %region_18.19_spmd} | conditional | flops 271122688 | bytes 10255450 | solution.py:335
  406.0 2.4 fusion.37
  409.4 2.1 fusion.42
  411.6 1.8 fusion.43
  413.4 8.6 %conditional.19 = ((f32[256,4,128]{2,0,1:T(8,128)S(1)}, f32[256,4,128]{2,0,1:T(8,128)S(1)})) conditional(s32[]{:T(128)} %convert_element_type.268, (s32[256]{0:T(256)S(1)}, s32[]{:T(128)}, s32[256]{0:T(256)S(1)}, s32[4096]{0:T(1024)}, bf16[256,4,128]{0,2,1:T(8,128)(2,1)}, /*index=5*/bf16[256,4,128]{0,2,1:T(8,128)(2,1)}, f32[4,4096]{1,0:T(4,128)}, ...), branch_computations={%region_19.20_spmd, %region_20.21_spmd} | conditional | flops 271122688 | bytes 7109702 | solution.py:335
  415.7 2.5 fusion.50
  418.2 2.1 fusion.55
  420.3 1.7 fusion.56
  422.0 8.6 %conditional.20 = ((f32[256,4,128]{2,0,1:T(8,128)S(1)}, f32[256,4,128]{2,0,1:T(8,128)S(1)})) conditional(s32[]{:T(128)} %convert_element_type.267, (s32[256]{0:T(256)S(1)}, s32[]{:T(128)}, s32[256]{0:T(256)S(1)}, s32[4096]{0:T(1024)}, bf16[256,4,128]{0,2,1:T(8,128)(2,1)}, /*index=5*/bf16[256,4,128]{0,2,1:T(8,128)(2,1)}, f32[4,4096]{1,0:T(4,128)}, ...), branch_computations={%region_21.22_spmd, %region_22.23_spmd} | conditional | flops 271122688 | bytes 7109702 | solution.py:335
  424.3 2.5 fusion.63
  426.8 2.1 fusion.68
  428.9 1.7 fusion.69
  430.6 8.8 %conditional.21 = ((f32[256,4,128]{2,0,1:T(8,128)S(1)}, f32[256,4,128]{2,0,1:T(8,128)S(1)})) conditional(s32[]{:T(128)} %convert_element_type.266, (s32[256]{0:T(256)S(1)}, s32[]{:T(128)}, s32[256]{0:T(256)S(1)}, s32[4096]{0:T(1024)}, bf16[256,4,128]{0,2,1:T(8,128)(2,1)}, /*index=5*/bf16[256,4,128]{0,2,1:T(8,128)(2,1)}, f32[4,4096]{1,0:T(4,128)}, ...), branch_computations={%region_23.24_spmd, %region_24.25_spmd} | conditional | flops 271122688 | bytes 7109702 | solution.py:335
  433.2 2.5 fusion.76
  435.7 2.1 fusion.81
  437.8 1.7 fusion.82
  439.5 8.6 %conditional.22 = ((f32[256,4,128]{2,0,1:T(8,128)S(1)}, f32[256,4,128]{2,0,1:T(8,128)S(1)})) conditional(s32[]{:T(128)} %convert_element_type.265, (s32[256]{0:T(256)S(1)}, s32[]{:T(128)}, s32[256]{0:T(256)S(1)}, s32[4096]{0:T(1024)}, bf16[256,4,128]{0,2,1:T(8,128)(2,1)}, /*index=5*/bf16[256,4,128]{0,2,1:T(8,128)(2,1)}, f32[4,4096]{1,0:T(4,128)}, ...), branch_computations={%region_25.26_spmd, %region_26.27_spmd} | conditional | flops 271122688 | bytes 7109702 | solution.py:335
  441.8 2.5 fusion.89
  444.3 2.1 fusion.94
  446.4 1.7 fusion.95
  448.1 8.6 %conditional.23 = ((f32[256,4,128]{2,0,1:T(8,128)S(1)}, f32[256,4,128]{2,0,1:T(8,128)S(1)})) conditional(s32[]{:T(128)} %convert_element_type.264, (s32[256]{0:T(256)S(1)}, s32[]{:T(128)}, s32[256]{0:T(256)S(1)}, s32[4096]{0:T(1024)}, bf16[256,4,128]{0,2,1:T(8,128)(2,1)}, /*index=5*/bf16[256,4,128]{0,2,1:T(8,128)(2,1)}, f32[4,4096]{1,0:T(4,128)}, ...), branch_computations={%region_27.28_spmd, %region_28.29_spmd} | conditional | flops 271122688 | bytes 7109702 | solution.py:335
  450.4 2.5 fusion.102
  452.9 2.1 fusion.107
  456.7 8.6 %conditional.24 = ((f32[256,4,128]{2,0,1:T(8,128)S(1)}, f32[256,4,128]{2,0,1:T(8,128)S(1)})) conditional(s32[]{:T(128)} %convert_element_type.263, (s32[256]{0:T(256)S(1)}, s32[]{:T(128)}, s32[256]{0:T(256)S(1)}, s32[4096]{0:T(1024)}, bf16[256,4,128]{0,2,1:T(8,128)(2,1)}, /*index=5*/bf16[256,4,128]{0,2,1:T(8,128)(2,1)}, f32[4,4096]{1,0:T(4,128)}, ...), branch_computations={%region_29.30_spmd, %region_30.31_spmd} | conditional | flops 271122688 | bytes 7109702 | solution.py:335
  459.0 2.5 fusion.115
  461.6 2.1 fusion.120
  465.4 8.6 %conditional.25 = ((f32[256,4,128]{2,0,1:T(8,128)S(1)}, f32[256,4,128]{2,0,1:T(8,128)S(1)})) conditional(s32[]{:T(128)} %convert_element_type.262, (s32[256]{0:T(256)S(1)}, s32[]{:T(128)}, s32[256]{0:T(256)S(1)}, s32[4096]{0:T(1024)}, bf16[256,4,128]{0,2,1:T(8,128)(2,1)}, /*index=5*/bf16[256,4,128]{0,2,1:T(8,128)(2,1)}, f32[4,4096]{1,0:T(4,128)}, ...), branch_computations={%region_31.32_spmd, %region_32.33_spmd} | conditional | flops 271122688 | bytes 7109702 | solution.py:335
  467.7 2.5 fusion.128
  470.2 2.1 fusion.133
  474.1 7.6 %conditional.26 = (bf16[256,512]{1,0:T(8,128)(2,1)S(1)}, bf16[256,512]{1,0:T(8,128)(2,1)S(1)}) conditional(s32[]{:T(128)} %convert_element_type.261, (s32[256]{0:T(256)S(1)}, s32[]{:T(128)}, s32[256]{0:T(256)S(1)}, s32[4096]{0:T(1024)}, bf16[256,512]{0,1:T(8,128)(2,1)}, /*index=5*/bf16[256,4,128]{0,2,1:T(8,128)(2,1)}, f32[4,4096]{1,0:T(4,128)}, ...), branch_computations={%region_33.34_spmd, %region_34.35_spmd} | conditional | flops 271384832 | bytes 10779738
  482.5 92.8 %while.45 = (s32[]{:T(128)}, f32[4,128,128]{2,1,0:T(8,128)S(1)}, f32[]{:T(128)}, s32[]{:T(128)}, f32[16]{0:T(128)S(1)}, /*index=5*/f32[16]{0:T(128)S(1)}, f32[16...) while((s32[]{:T(128)}, f32[4,128,128]{2,1,0:T(8,128)S(1)}, ...), condition=%wide.region_1.2_spmd, body=%wide.region_0.1_spmd.sunk | while | flops 262154 | bytes 786708 | solution.py:22
  (361 shorter events, 131.6 us)
Async XLA Ops:
  7.2 53.5 %copy-start = (bf16[256,512]{1,0:T(8,128)(2,1)S(1)}, bf16[256,512]{1,0:T(8,128)(2,1)}, u32[]{:S(2)}) copy-start(bf16[256,512]{1,0:T(8,128)(2,1)} %param.43) | copy-start | bytes 786436
  7.2 12.1 %copy-start.32 = (f32[4]{0:T(128)S(1)}, f32[4]{0:T(128)}, u32[]{:S(2)}) copy-start(f32[4]{0:T(128)} %param.44) | copy-start | bytes 52
  7.2 8.8 %copy-start.22 = (bf16[256,512]{1,0:T(8,128)(2,1)S(1)}, bf16[256,512]{1,0:T(8,128)(2,1)}, u32[]{:S(2)}) copy-start(bf16[256,512]{1,0:T(8,128)(2,1)} %param.48) | copy-start | bytes 786436
  7.2 9.8 %copy-start.23 = (bf16[256,512]{1,0:T(8,128)(2,1)S(1)}, bf16[256,512]{1,0:T(8,128)(2,1)}, u32[]{:S(2)}) copy-start(bf16[256,512]{1,0:T(8,128)(2,1)} %param.47) | copy-start | bytes 786436
  7.2 35.9 %copy-start.12 = (bf16[256,512]{1,0:T(8,128)(2,1)S(1)}, bf16[256,512]{1,0:T(8,128)(2,1)}, u32[]{:S(2)}) copy-start(bf16[256,512]{1,0:T(8,128)(2,1)} %param.42) | copy-start | bytes 786436
  7.2 52.0 %all-gather.14.cloned.1.call-start = ((), (), s32[]{:S(2)}) async-start(), calls=%async_computation.4 | async-start | bytes 4456448 | tf_op jit(solution)/shard_map/all_gather | solution.py:13
  7.3 35.9 %copy-start.34 = (f32[256]{0:T(256)}, f32[256]{0:T(256)S(1)}, u32[]{:S(2)}) copy-start(f32[256]{0:T(256)S(1)} %convert_negate_fusion) | copy-start | bytes 3076
  13.0 202.8 %copy-start.7 = (bf16[256,512]{0,1:T(8,128)(2,1)}, bf16[256,512]{0,1:T(8,128)(2,1)S(1)}, u32[]{:S(2)}) copy-start(bf16[256,512]{0,1:T(8,128)(2,1)S(1)} %copy.872) | copy-start | bytes 786436
  14.2 152.9 %copy-start.9 = (bf16[256,512]{0,1:T(8,128)(2,1)}, bf16[256,512]{0,1:T(8,128)(2,1)S(1)}, u32[]{:S(2)}) copy-start(bf16[256,512]{0,1:T(8,128)(2,1)S(1)} %copy.873) | copy-start | bytes 786436
  16.0 169.6 %all-gather.10.cloned.1.call-start = ((), (), s32[]{:S(2)}) async-start(), calls=%async_computation.2 | async-start | bytes 4456448 | tf_op jit(solution)/shard_map/all_gather | solution.py:180
  16.9 168.7 %all-gather.8.cloned.1.call-start = ((), (), s32[]{:S(2)}) async-start(), calls=%async_computation.1 | async-start | bytes 4456448 | tf_op jit(solution)/shard_map/all_gather | solution.py:179
  17.8 463.9 %all-gather.12.cloned.1.call-start = ((), (), s32[]{:S(2)}) async-start(), calls=%async_computation.3 | async-start | bytes 4456448 | tf_op jit(solution)/shard_map/all_gather | solution.py:13
  43.2 17.5 %copy-start.13 = (bf16[256,512]{0,1:T(8,128)(2,1)}, bf16[256,512]{0,1:T(8,128)(2,1)S(1)}, u32[]{:S(2)}) copy-start(bf16[256,512]{0,1:T(8,128)(2,1)S(1)} %copy.902) | copy-start | bytes 786436
  59.3 0.7 copy-start.21
  59.3 2.4 copy-start.24
  59.3 24.6 %copy-start.25 = (bf16[256,512]{1,0:T(8,128)(2,1)S(1)}, bf16[256,512]{1,0:T(8,128)(2,1)}, u32[]{:S(2)}) copy-start(bf16[256,512]{1,0:T(8,128)(2,1)} %param.46) | copy-start | bytes 786436
  59.3 0.6 copy-start.36
  59.4 107.7 %copy-start.31 = (f32[16,4]{1,0:T(8,128)}, f32[16,4]{1,0:T(8,128)S(1)}, u32[]{:S(2)}) copy-start(f32[16,4]{1,0:T(8,128)S(1)} %get-tuple-element.3290) | copy-start | bytes 772
  59.4 108.1 %copy-start.38 = (f32[16]{0:T(128)}, f32[16]{0:T(128)S(1)}, u32[]{:S(2)}) copy-start(f32[16]{0:T(128)S(1)} %get-tuple-element.3292) | copy-start | bytes 196
  62.6 147.3 %collective-permute-start.15 = (bf16[256,512]{0,1:T(8,128)(2,1)}, bf16[256,512]{0,1:T(8,128)(2,1)}, u32[]{:S(2)}, u32[]{:S(2)}) collective-permute-start(bf16[256,512]{0,1:T(8,128)(2,1)} %copy.720), channel_id=1, source_target_pairs={{8,0},{16,8},{24,16},{32,24},{40,32},{48,40},{56,48},{64,56},{72,6... | collective-permute-start | bytes 786440 | tf_op jit(solution)/shard_map/ppermute | solution.py:28
  71.0 157.9 %collective-permute-start.13 = (bf16[256,512]{0,1:T(8,128)(2,1)}, bf16[256,512]{0,1:T(8,128)(2,1)}, u32[]{:S(2)}, u32[]{:S(2)}) collective-permute-start(bf16[256,512]{0,1:T(8,128)(2,1)} %copy.720), channel_id=1, source_target_pairs={{16,0},{24,8},{32,16},{40,24},{48,32},{56,40},{64,48},{72,56},{80,... | collective-permute-start | bytes 786440 | tf_op jit(solution)/shard_map/ppermute | solution.py:28
  84.8 132.1 %collective-permute-start.14 = (bf16[256,512]{0,1:T(8,128)(2,1)}, bf16[256,512]{0,1:T(8,128)(2,1)}, u32[]{:S(2)}, u32[]{:S(2)}) collective-permute-start(bf16[256,512]{0,1:T(8,128)(2,1)} %copy.716), channel_id=1, source_target_pairs={{8,0},{16,8},{24,16},{32,24},{40,32},{48,40},{56,48},{64,56},{72,6... | collective-permute-start | bytes 786440 | tf_op jit(solution)/shard_map/ppermute | solution.py:28
  94.1 136.7 %collective-permute-start.12 = (bf16[256,512]{0,1:T(8,128)(2,1)}, bf16[256,512]{0,1:T(8,128)(2,1)}, u32[]{:S(2)}, u32[]{:S(2)}) collective-permute-start(bf16[256,512]{0,1:T(8,128)(2,1)} %copy.716), channel_id=1, source_target_pairs={{16,0},{24,8},{32,16},{40,24},{48,32},{56,40},{64,48},{72,56},{80,... | collective-permute-start | bytes 786440 | tf_op jit(solution)/shard_map/ppermute | solution.py:28
  107.5 125.4 %collective-permute-start.11 = (bf16[256,512]{0,1:T(8,128)(2,1)}, bf16[256,512]{0,1:T(8,128)(2,1)S(1)}, u32[]{:S(2)}, u32[]{:S(2)}) collective-permute-start(bf16[256,512]{0,1:T(8,128)(2,1)} %copy.720), channel_id=1, source_target_pairs={{24,0},{32,8},{40,16},{48,24},{56,32},{64,40},{72,48},{80,56},{88,... | collective-permute-start | bytes 786440 | tf_op jit(solution)/shard_map/ppermute | solution.py:28
  127.7 54.4 %all-to-all-start = ((s32[16,1,256]{2,1,0:T(1,128)}), s32[16,1,256]{2,1,0:T(1,128)}, u32[]{:S(2)}, u32[]{:S(2)}) async-start(s32[16,1,256]{2,1,0:T(1,128)} %stack.2), calls=%async_computation | async-start | bytes 32768 | tf_op jit(solution)/shard_map/all_to_all | solution.py:89
  167.5 48.4 %copy-start.5 = (f32[4,256,256]{2,1,0:T(8,128)}, f32[4,256,256]{2,1,0:T(8,128)S(1)}, u32[]{:S(2)}) copy-start(f32[4,256,256]{2,1,0:T(8,128)S(1)} %convolution_multiply_fusion.9) | copy-start | bytes 3145732
  208.9 52.5 %copy-start.16 = (f32[256,4]{1,0:T(8,128)}, f32[256,4]{1,0:T(8,128)S(1)}, u32[]{:S(2)}) copy-start(f32[256,4]{1,0:T(8,128)S(1)} %copy.870) | copy-start | bytes 12292
  209.9 25.0 %collective-permute-start.10 = (bf16[256,512]{0,1:T(8,128)(2,1)}, bf16[256,512]{0,1:T(8,128)(2,1)S(1)}, u32[]{:S(2)}, u32[]{:S(2)}) collective-permute-start(bf16[256,512]{0,1:T(8,128)(2,1)} %copy.716), channel_id=1, source_target_pairs={{24,0},{32,8},{40,16},{48,24},{56,32},{64,40},{72,48},{80,56},{88,... | collective-permute-start | bytes 786440 | tf_op jit(solution)/shard_map/ppermute | solution.py:28
  216.9 77.6 %collective-permute-start.9 = (bf16[256,512]{0,1:T(8,128)(2,1)}, bf16[256,512]{0,1:T(8,128)(2,1)}, u32[]{:S(2)}, u32[]{:S(2)}) collective-permute-start(bf16[256,512]{0,1:T(8,128)(2,1)} %copy.720), channel_id=1, source_target_pairs={{32,0},{40,8},{48,16},{56,24},{64,32},{72,40},{80,48},{88,56},{96,... | collective-permute-start | bytes 786440 | tf_op jit(solution)/shard_map/ppermute | solution.py:28
  228.9 96.9 %collective-permute-start.8 = (bf16[256,512]{0,1:T(8,128)(2,1)}, bf16[256,512]{0,1:T(8,128)(2,1)}, u32[]{:S(2)}, u32[]{:S(2)}) collective-permute-start(bf16[256,512]{0,1:T(8,128)(2,1)} %copy.716), channel_id=1, source_target_pairs={{32,0},{40,8},{48,16},{56,24},{64,32},{72,40},{80,48},{88,56},{96,... | collective-permute-start | bytes 786440 | tf_op jit(solution)/shard_map/ppermute | solution.py:28
  230.9 96.9 %collective-permute-start.7 = (bf16[256,512]{0,1:T(8,128)(2,1)}, bf16[256,512]{0,1:T(8,128)(2,1)}, u32[]{:S(2)}, u32[]{:S(2)}) collective-permute-start(bf16[256,512]{0,1:T(8,128)(2,1)} %copy.720), channel_id=1, source_target_pairs={{40,0},{48,8},{56,16},{64,24},{72,32},{80,40},{88,48},{96,56},{104... | collective-permute-start | bytes 786440 | tf_op jit(solution)/shard_map/ppermute | solution.py:28
  232.9 28.5 %copy-start.20 = (bf16[256,512]{0,1:T(8,128)(2,1)}, bf16[256,512]{0,1:T(8,128)(2,1)S(1)}, u32[]{:S(2)}) copy-start(bf16[256,512]{0,1:T(8,128)(2,1)S(1)} %collective-permute-done.11) | copy-start | bytes 786436
  232.9 96.8 %collective-permute-start.6 = (bf16[256,512]{0,1:T(8,128)(2,1)}, bf16[256,512]{0,1:T(8,128)(2,1)}, u32[]{:S(2)}, u32[]{:S(2)}) collective-permute-start(bf16[256,512]{0,1:T(8,128)(2,1)} %copy.716), channel_id=1, source_target_pairs={{40,0},{48,8},{56,16},{64,24},{72,32},{80,40},{88,48},{96,56},{104... | collective-permute-start | bytes 786440 | tf_op jit(solution)/shard_map/ppermute | solution.py:28
  234.9 26.5 %copy-start.28 = (bf16[256,512]{0,1:T(8,128)(2,1)}, bf16[256,512]{0,1:T(8,128)(2,1)S(1)}, u32[]{:S(2)}) copy-start(bf16[256,512]{0,1:T(8,128)(2,1)S(1)} %collective-permute-done.10) | copy-start | bytes 786436
  234.9 96.9 %collective-permute-start.5 = (bf16[256,512]{0,1:T(8,128)(2,1)}, bf16[256,512]{0,1:T(8,128)(2,1)}, u32[]{:S(2)}, u32[]{:S(2)}) collective-permute-start(bf16[256,512]{0,1:T(8,128)(2,1)} %copy.720), channel_id=1, source_target_pairs={{48,0},{56,8},{64,16},{72,24},{80,32},{88,40},{96,48},{104,56},{11... | collective-permute-start | bytes 786440 | tf_op jit(solution)/shard_map/ppermute | solution.py:28
  283.1 3.0 copy-start.29
  289.3 44.4 %copy-start.3 = (f32[4,256,256]{2,1,0:T(8,128)S(1)}, f32[4,256,256]{2,1,0:T(8,128)}, u32[]{:S(2)}) copy-start(f32[4,256,256]{2,1,0:T(8,128)} %convolution_multiply_fusion.10) | copy-start | bytes 3145732
  289.3 44.4 %copy-start.10 = (bf16[256,512]{0,1:T(8,128)(2,1)S(1)}, bf16[256,512]{0,1:T(8,128)(2,1)}, u32[]{:S(2)}) copy-start(bf16[256,512]{0,1:T(8,128)(2,1)} %copy-done.9) | copy-start | bytes 786436
  291.3 43.6 %copy-start.19 = (bf16[4,256,128]{1,2,0:T(8,128)(2,1)S(1)}, bf16[4,256,128]{1,2,0:T(8,128)(2,1)}, u32[]{:S(2)}) copy-start(bf16[4,256,128]{1,2,0:T(8,128)(2,1)} %get-tuple-element.2722) | copy-start | bytes 786436
  293.2 42.7 %copy-start.17 = (f32[256,4]{1,0:T(8,128)S(1)}, f32[256,4]{1,0:T(8,128)}, u32[]{:S(2)}) copy-start(f32[256,4]{1,0:T(8,128)} %copy-done.16) | copy-start | bytes 12292
  294.5 162.2 %collective-permute-start.4 = (bf16[256,512]{0,1:T(8,128)(2,1)}, bf16[256,512]{0,1:T(8,128)(2,1)}, u32[]{:S(2)}, u32[]{:S(2)}) collective-permute-start(bf16[256,512]{0,1:T(8,128)(2,1)} %copy.716), channel_id=1, source_target_pairs={{48,0},{56,8},{64,16},{72,24},{80,32},{88,40},{96,48},{104,56},{11... | collective-permute-start | bytes 786440 | tf_op jit(solution)/shard_map/ppermute | solution.py:28
  325.8 139.6 %collective-permute-start.3 = (bf16[256,512]{0,1:T(8,128)(2,1)}, bf16[256,512]{0,1:T(8,128)(2,1)}, u32[]{:S(2)}, u32[]{:S(2)}) collective-permute-start(bf16[256,512]{0,1:T(8,128)(2,1)} %copy.720), channel_id=1, source_target_pairs={{56,0},{64,8},{72,16},{80,24},{88,32},{96,40},{104,48},{112,56},{1... | collective-permute-start | bytes 786440 | tf_op jit(solution)/shard_map/ppermute | solution.py:28
  327.7 137.6 %collective-permute-start.2 = (bf16[256,512]{0,1:T(8,128)(2,1)}, bf16[256,512]{0,1:T(8,128)(2,1)}, u32[]{:S(2)}, u32[]{:S(2)}) collective-permute-start(bf16[256,512]{0,1:T(8,128)(2,1)} %copy.716), channel_id=1, source_target_pairs={{56,0},{64,8},{72,16},{80,24},{88,32},{96,40},{104,48},{112,56},{1... | collective-permute-start | bytes 786440 | tf_op jit(solution)/shard_map/ppermute | solution.py:28
  329.7 144.3 %collective-permute-start.1 = (bf16[256,512]{0,1:T(8,128)(2,1)}, bf16[256,512]{0,1:T(8,128)(2,1)}, u32[]{:S(2)}, u32[]{:S(2)}) collective-permute-start(bf16[256,512]{0,1:T(8,128)(2,1)} %copy.720), channel_id=1, source_target_pairs={{64,0},{72,8},{80,16},{88,24},{96,32},{104,40},{112,48},{120,56},{... | collective-permute-start | bytes 786440 | tf_op jit(solution)/shard_map/ppermute | solution.py:28
  331.7 142.3 %collective-permute-start = (bf16[256,512]{0,1:T(8,128)(2,1)}, bf16[256,512]{0,1:T(8,128)(2,1)}, u32[]{:S(2)}, u32[]{:S(2)}) collective-permute-start(bf16[256,512]{0,1:T(8,128)(2,1)} %copy.716), channel_id=1, source_target_pairs={{64,0},{72,8},{80,16},{88,24},{96,32},{104,40},{112,48},{120,56},{... | collective-permute-start | bytes 786440 | tf_op jit(solution)/shard_map/ppermute | solution.py:28
  334.1 48.7 %copy-start.30 = (f32[4,256]{1,0:T(4,128)S(1)}, f32[4,256]{1,0:T(4,128)}, u32[]{:S(2)}) copy-start(f32[4,256]{1,0:T(4,128)} %get-tuple-element.3289) | copy-start | bytes 12292
  334.1 69.5 %copy-start.1 = (bf16[256,512]{0,1:T(8,128)(2,1)S(1)}, bf16[256,512]{0,1:T(8,128)(2,1)}, u32[]{:S(2)}) copy-start(bf16[256,512]{0,1:T(8,128)(2,1)} %copy.717) | copy-start | bytes 786436
  334.1 69.5 %copy-start.18 = (bf16[256,512]{0,1:T(8,128)(2,1)S(1)}, bf16[256,512]{0,1:T(8,128)(2,1)}, u32[]{:S(2)}) copy-start(bf16[256,512]{0,1:T(8,128)(2,1)} %copy.715) | copy-start | bytes 786436
  404.6 3.8 copy-start.15
  474.0 7.7 %copy-start.37 = (f32[16]{0:T(128)S(1)}, f32[16]{0:T(128)}, u32[]{:S(2)}) copy-start(f32[16]{0:T(128)} %copy-done.36) | copy-start | bytes 196
  474.0 7.7 %copy-start.39 = (f32[16]{0:T(128)S(1)}, f32[16]{0:T(128)}, u32[]{:S(2)}) copy-start(f32[16]{0:T(128)} %copy-done.38) | copy-start | bytes 196
  475.6 2.5 copy-start.2
  481.7 0.7 copy-start.26
  481.7 0.8 copy-start.27
  481.8 93.6 %copy-start.33 = (f32[4]{0:T(128)S(1)}, f32[4]{0:T(128)}, u32[]{:S(2)}) copy-start(f32[4]{0:T(128)} %param.44) | copy-start | bytes 52
  481.8 93.6 %copy-start.35 = (f32[256]{0:T(256)S(1)}, f32[256]{0:T(256)}, u32[]{:S(2)}) copy-start(f32[256]{0:T(256)} %copy-done.34) | copy-start | bytes 3076
  481.8 93.6 %copy-start.11 = (bf16[256,512]{0,1:T(8,128)(2,1)S(1)}, bf16[256,512]{0,1:T(8,128)(2,1)}, u32[]{:S(2)}) copy-start(bf16[256,512]{0,1:T(8,128)(2,1)} %copy-done.9) | copy-start | bytes 786436
  481.8 94.0 %copy-start.8 = (bf16[256,512]{0,1:T(8,128)(2,1)S(1)}, bf16[256,512]{0,1:T(8,128)(2,1)}, u32[]{:S(2)}) copy-start(bf16[256,512]{0,1:T(8,128)(2,1)} %copy-done.7) | copy-start | bytes 786436
  575.3 1.2 copy-start.6
  575.3 1.3 copy-start.14
  575.8 2.1 copy-start.4
Sparse Core Ops, SparseCore 0:
  16.1 43.1 all-gather.13
  61.3 50.4 all-gather.9
  114.4 61.3 all-gather.7
  178.4 46.6 all-gather.11
